TPU v7x, 128 devices: a whole 4x4x4 slice. The times are simulated.
128 devices in a mesh: dp: 4 (over x), expert: 32 (over y, z, core).
Axes of the slice: x: 4, y: 4, z: 4, core: 2. Of those that a mesh axis runs over, the one named last changes fastest.
Arguments:
- tokens: bfloat16 [16384, 4096], P(('dp', 'expert')), may hold values from -6 to 6
- cotangent: bfloat16 [16384, 4096], P(('dp', 'expert')), may hold values from -6 to 6
- routes: int32 [16384], P(('dp', 'expert')), may hold values from 0 to 31, as said below
- combine: float32 [16384], P(('dp', 'expert')), may hold values from 0.05 to 1
- expert_weights: bfloat16 [32, 3, 1536, 4096], P('expert', None, 'dp'), may hold values from -0.09375 to 0.09375
Outputs:
- combined: bfloat16 [16384, 4096], P(('dp', 'expert'))
- token_grad: bfloat16 [16384, 4096], P(('dp', 'expert'))
- combine_grad: float32 [16384], P(('dp', 'expert'))
Inputs may be any that keep to these rules, and one draw needn't show every extreme that they name: `routes`: among the 128 rows of every device, two experts, the same two on every device, are each named by exactly 8 rows, and every other expert by 3 or 4 rows.
All inputs are finite; a program needn't handle non-finite values.
Results may differ from a plain program's by a relative error of at most 0.015.
Values may be sent and summed in bfloat16 or wider, within the bound.
No kernel may reach another device: no remote copies, remote signals or barrier semaphores. Data moves between devices by JAX's collectives and lax.ppermute only.
A program may use at most 192 MiB of HBM per device.

v0:
```python
import jax
import jax.numpy as jnp
from jax import lax
from jax.sharding import PartitionSpec as P


def placement(member, slot_count):
    within = jnp.sum((jnp.cumsum(member, 0) - 1) * member, 1)
    owner_group = jnp.sum(member * lax.iota(jnp.int32, member.shape[1])[None, :], 1)
    is_used = jnp.sum(member, 1) > 0
    target = owner_group * slot_count + within
    buffer_cells = lax.iota(jnp.int32, member.shape[1] * slot_count)
    return ((buffer_cells[:, None] == target[None, :]) & is_used[None, :]).astype(jnp.bfloat16)


def spread(layout, row_block):
    return jnp.dot(layout, row_block, preferred_element_type=jnp.float32).astype(jnp.bfloat16)


def collect(layout, buffer_rows):
    return lax.dot_general(
        layout, buffer_rows, (((0,), (0,)), ((), ())), preferred_element_type=jnp.float32
    )


def group_rows(values):
    return lax.all_gather(values, "dp", axis=0, tiled=True)


def group_sum(values):
    return lax.psum_scatter(values.astype(jnp.bfloat16), "dp", scatter_dimension=0, tiled=True)


def exchange(rows, experts, model_width):
    return lax.all_to_all(
        rows.reshape(experts, -1, model_width), "expert", split_axis=0, concat_axis=0, tiled=True
    ).reshape(-1, model_width)


def forward_rows(row_block, matrices):
    gate_up = jnp.einsum("rd,kfd->krf", row_block, matrices[:2], preferred_element_type=jnp.float32)
    gate_act = gate_up[0]
    up_act = gate_up[1]
    hidden = (gate_act * jax.nn.sigmoid(gate_act) * up_act).astype(jnp.bfloat16)
    partial_out = jnp.dot(hidden, matrices[2], preferred_element_type=jnp.float32)
    return (gate_act, up_act, partial_out)


def backward_rows(row_block, gate_act, up_act, matrices):
    hidden_grad = lax.dot_general(
        row_block, matrices[2], (((1,), (1,)), ((), ())), preferred_element_type=jnp.float32
    )
    squashed = jax.nn.sigmoid(gate_act)
    gate_grad = (hidden_grad * up_act * squashed * (1.0 + gate_act * (1.0 - squashed))).astype(
        jnp.bfloat16
    )
    up_grad = (hidden_grad * gate_act * squashed).astype(jnp.bfloat16)
    both_grads = jnp.stack([gate_grad, up_grad])
    return jnp.einsum("krf,kfd->rd", both_grads, matrices[:2], preferred_element_type=jnp.float32)


def shards(tokens, cotangent, routes, combine, expert_weights):
    weights = expert_weights[0]
    tok_dev = tokens.shape[0]
    model_width = tokens.shape[1]
    experts = lax.axis_size("expert")
    capacity = 2 * tok_dev // experts
    chunks = 2
    chunk_slots = capacity // chunks
    labels = lax.iota(jnp.int32, experts)
    member = (routes[:, None] == labels[None, :]).astype(jnp.int32)
    layout = placement(member, capacity).reshape(experts, capacity, tok_dev)
    cotangent_wide = cotangent.astype(jnp.float32)
    out_grad = (combine[:, None] * cotangent_wide).astype(jnp.bfloat16)
    layouts = [
        layout[:, c * chunk_slots : (c + 1) * chunk_slots].reshape(-1, tok_dev)
        for c in range(chunks)
    ]
    tok_in = [group_rows(exchange(spread(lay, tokens), experts, model_width)) for lay in layouts]
    cot_in = [group_rows(exchange(spread(lay, out_grad), experts, model_width)) for lay in layouts]
    expert_out = None
    input_grad = None
    for c in range(chunks):
        gate_act, up_act, part = forward_rows(tok_in[c], weights)
        out_back = exchange(group_sum(part), experts, model_width)
        piece = collect(layouts[c], out_back)
        expert_out = piece if expert_out is None else expert_out + piece
        grad_part = backward_rows(cot_in[c], gate_act, up_act, weights)
        grad_back = exchange(group_sum(grad_part), experts, model_width)
        piece = collect(layouts[c], grad_back)
        input_grad = piece if input_grad is None else input_grad + piece
    combined = (combine[:, None] * expert_out).astype(jnp.bfloat16)
    combine_grad = jnp.sum(expert_out * cotangent_wide, 1)
    token_grad = input_grad.astype(jnp.bfloat16)
    return (combined, token_grad, combine_grad)


def solution(mesh):
    return jax.shard_map(
        shards,
        mesh=mesh,
        in_specs=(
            P(("dp", "expert"), None),
            P(("dp", "expert"), None),
            P(("dp", "expert")),
            P(("dp", "expert")),
            P("expert", None, "dp", None),
        ),
        out_specs=(P(("dp", "expert"), None), P(("dp", "expert"), None), P(("dp", "expert"))),
        check_vma=False,
    )
```

profile of v0, /device:TPU:1, one launch (start us, length us, event | category | flops | bytes accessed | tf_op | source)
XLA Modules:
  0.0 472.8 jit_solution(6738018536119864457)
XLA Ops:
  7.2 0.8 fusion.73
  8.2 0.9 fusion.74
  9.3 1.4 convolution_convert_fusion.4
  10.7 1.5 reshape.93
  12.2 26.4 %all_to_all.40 = bf16[32,4,4096]{2,1,0:T(4,128)(2,1)} all-to-all(bf16[32,4,4096]{2,1,0:T(4,128)(2,1)S(1)} %reshape.93), channel_id=1, replica_groups=mesh['dp'=4,'expert'=32] {'expert'}, dimensions={0} | all-to-all | bytes 2097152 | tf_op jit(solution)/shard_map/all_to_all | solution.py:35
  38.7 2.1 reshape.94
  40.9 0.5 convolution_convert_fusion.2
  41.4 1.2 reshape.99
  42.6 20.9 %all_to_all.41 = bf16[32,4,4096]{2,1,0:T(4,128)(2,1)S(1)} all-to-all(bf16[32,4,4096]{2,1,0:T(4,128)(2,1)} %reshape.99), channel_id=1, replica_groups=mesh['dp'=4,'expert'=32] {'expert'}, dimensions={0} | all-to-all | bytes 2097152 | tf_op jit(solution)/shard_map/all_to_all | solution.py:35
  63.5 1.1 reshape.100
  64.7 0.4 convolution_convert_fusion.5
  65.1 0.4 reshape.89
  65.6 20.7 %all_to_all.42 = bf16[32,4,4096]{2,1,0:T(4,128)(2,1)S(1)} all-to-all(bf16[32,4,4096]{2,1,0:T(4,128)(2,1)S(1)} %reshape.89), channel_id=1, replica_groups=mesh['dp'=4,'expert'=32] {'expert'}, dimensions={0} | all-to-all | bytes 2097152 | tf_op jit(solution)/shard_map/all_to_all | solution.py:35
  86.2 1.1 reshape.90
  87.4 0.5 convolution_convert_fusion.3
  87.9 0.4 reshape.96
  88.3 20.7 %all_to_all.43 = bf16[32,4,4096]{2,1,0:T(4,128)(2,1)S(1)} all-to-all(bf16[32,4,4096]{2,1,0:T(4,128)(2,1)S(1)} %reshape.96), channel_id=1, replica_groups=mesh['dp'=4,'expert'=32] {'expert'}, dimensions={0} | all-to-all | bytes 2097152 | tf_op jit(solution)/shard_map/all_to_all | solution.py:35
  109.0 1.1 reshape.97
  110.2 8.8 %fusion.32 = f32[2,512,384]{2,1,0:T(8,128)} fusion(bf16[1,3,384,4096]{3,2,1,0:T(8,128)(2,1)} %param.9, bf16[512,4096]{1,0:T(8,128)(2,1)} %all-gather.7.cloned.1.call-done), kind=kOutput, calls=%fused_computation.43 | convolution fusion | flops 3221225472 | bytes 12058624 | tf_op jit(solution)/shard_map/rd,kfd->krf/dot_general | solution.py:41
  119.0 18.0 %all-gather.11.cloned.1.call-done = bf16[512,4096]{1,0:T(8,128)(2,1)} async-done(((bf16[128,4096]{1,0:T(8,128)(2,1)}), bf16[512,4096]{1,0:T(8,128)(2,1)}) %all-gather.11.cloned.1.call-update) | async-done | bytes 4194320 | tf_op jit(solution)/shard_map/all_gather | solution.py:27
  137.0 6.0 %fusion.72 = (bf16[1,512,384]{2,1,0:T(8,128)(2,1)S(1)}, bf16[1,512,384]{2,1,0:T(8,128)(2,1)S(1)}) fusion(f32[2,512,384]{2,1,0:T(8,128)} %fusion.32, bf16[512,4096]{1,0:T(8,128)(2,1)} %all-gather.11.cloned.1.call-done, bf16[1,3,384,4096]{3,2,1,0:T(8,128)(2,1)} %param.9), kind=kOutput, calls=%fused_computation.87 | convolution fusion | flops 1613168640 | bytes 9699328 | tf_op jit(solution)/shard_map/dot_general | solution.py:50
  143.0 7.7 %bitcast_convert_fusion = bf16[512,4096]{1,0:T(8,128)(2,1)} fusion(bf16[1,3,384,4096]{3,2,1,0:T(8,128)(2,1)} %param.9, bf16[1,512,384]{2,1,0:T(8,128)(2,1)S(1)} %get-tuple-element.9, bf16[1,512,384]{2,1,0:T(8,128)(2,1)S(1)} %get-tuple-element.8), kind=kOutput, calls=%fused_computation | convolution fusion | flops 3223715840 | bytes 11272192 | tf_op jit(solution)/shard_map/krf,kfd->rd/dot_general | solution.py:59
  150.8 0.2 reduce-scatter.9.cloned.1.call-start
  151.0 36.9 %all-gather.5.cloned.1.call-done = bf16[512,4096]{1,0:T(8,128)(2,1)} async-done(((bf16[128,4096]{1,0:T(8,128)(2,1)}), bf16[512,4096]{1,0:T(8,128)(2,1)}) %all-gather.5.cloned.1.call-update) | async-done | bytes 4194320 | tf_op jit(solution)/shard_map/all_gather | solution.py:27
  187.9 8.7 %fusion.27 = f32[2,512,384]{2,1,0:T(8,128)} fusion(bf16[1,3,384,4096]{3,2,1,0:T(8,128)(2,1)} %param.9, bf16[512,4096]{1,0:T(8,128)(2,1)} %all-gather.5.cloned.1.call-done), kind=kOutput, calls=%fused_computation.42 | convolution fusion | flops 3221225472 | bytes 12058624 | tf_op jit(solution)/shard_map/rd,kfd->krf/dot_general | solution.py:41
  196.6 41.5 %all-gather.9.cloned.1.call-done = bf16[512,4096]{1,0:T(8,128)(2,1)} async-done(((bf16[128,4096]{1,0:T(8,128)(2,1)}), bf16[512,4096]{1,0:T(8,128)(2,1)}) %all-gather.9.cloned.1.call-update) | async-done | bytes 4194320 | tf_op jit(solution)/shard_map/all_gather | solution.py:27
  238.0 6.0 %fusion.71 = (bf16[1,512,384]{2,1,0:T(8,128)(2,1)S(1)}, bf16[1,512,384]{2,1,0:T(8,128)(2,1)S(1)}) fusion(f32[2,512,384]{2,1,0:T(8,128)} %fusion.27, bf16[512,4096]{1,0:T(8,128)(2,1)} %all-gather.9.cloned.1.call-done, bf16[1,3,384,4096]{3,2,1,0:T(8,128)(2,1)} %param.9), kind=kOutput, calls=%fused_computation.86 | convolution fusion | flops 1613168640 | bytes 9699328 | tf_op jit(solution)/shard_map/dot_general | solution.py:50
  244.0 7.7 %bitcast_convert_fusion.1 = bf16[512,4096]{1,0:T(8,128)(2,1)} fusion(bf16[1,3,384,4096]{3,2,1,0:T(8,128)(2,1)} %param.9, bf16[1,512,384]{2,1,0:T(8,128)(2,1)S(1)} %get-tuple-element.7, bf16[1,512,384]{2,1,0:T(8,128)(2,1)S(1)} %get-tuple-element.6), kind=kOutput, calls=%fused_computation.1 | convolution fusion | flops 3223715840 | bytes 11272192 | tf_op jit(solution)/shard_map/krf,kfd->rd/dot_general | solution.py:59
  251.8 6.7 %convolution_convert_fusion = bf16[512,4096]{1,0:T(8,128)(2,1)} fusion(bf16[1,3,384,4096]{3,2,1,0:T(8,128)(2,1)} %param.9, f32[2,512,384]{2,1,0:T(8,128)} %fusion.32), kind=kOutput, calls=%fused_computation.8 | convolution fusion | flops 1613889536 | bytes 8912896 | tf_op jit(solution)/shard_map/dot_general | solution.py:45
  258.6 6.8 %convolution_convert_fusion.1 = bf16[512,4096]{1,0:T(8,128)(2,1)} fusion(bf16[1,3,384,4096]{3,2,1,0:T(8,128)(2,1)} %param.9, f32[2,512,384]{2,1,0:T(8,128)} %fusion.27), kind=kOutput, calls=%fused_computation.9 | convolution fusion | flops 1613889536 | bytes 8912896 | tf_op jit(solution)/shard_map/dot_general | solution.py:45
  265.5 22.0 %reduce-scatter.11.cloned.1.call-done = bf16[128,4096]{1,0:T(8,128)(2,1)} async-done(((bf16[512,4096]{1,0:T(8,128)(2,1)}), bf16[128,4096]{1,0:T(8,128)(2,1)}) %reduce-scatter.11.cloned.1.call-update) | async-done | bytes 1048592 | tf_op jit(solution)/shard_map/reduce_scatter | solution.py:31
  287.5 2.2 reshape.101
  289.7 7.6 %all-to-all-start.7 = ((bf16[32,4,4096]{2,1,0:T(4,128)(2,1)}), bf16[32,4,4096]{2,1,0:T(4,128)(2,1)S(1)}, u32[]{:S(2)}, u32[]{:S(2)}) async-start(bf16[32,4,4096]{2,1,0:T(4,128)(2,1)} %reshape.101), calls=%async_computation.11 | async-start | bytes 2097152 | tf_op jit(solution)/shard_map/all_to_all | solution.py:35
  297.4 39.1 %reduce-scatter.9.cloned.1.call-done = bf16[128,4096]{1,0:T(8,128)(2,1)} async-done(((bf16[512,4096]{1,0:T(8,128)(2,1)}), bf16[128,4096]{1,0:T(8,128)(2,1)}) %reduce-scatter.9.cloned.1.call-update) | async-done | bytes 1048592 | tf_op jit(solution)/shard_map/reduce_scatter | solution.py:31
  336.5 2.2 reshape.98
  338.7 7.7 %all-to-all-start.5 = ((bf16[32,4,4096]{2,1,0:T(4,128)(2,1)}), bf16[32,4,4096]{2,1,0:T(4,128)(2,1)S(1)}, u32[]{:S(2)}, u32[]{:S(2)}) async-start(bf16[32,4,4096]{2,1,0:T(4,128)(2,1)} %reshape.98), calls=%async_computation.8 | async-start | bytes 2097152 | tf_op jit(solution)/shard_map/all_to_all | solution.py:35
  346.4 39.0 %reduce-scatter.7.cloned.1.call-done = bf16[128,4096]{1,0:T(8,128)(2,1)} async-done(((bf16[512,4096]{1,0:T(8,128)(2,1)}), bf16[128,4096]{1,0:T(8,128)(2,1)}) %reduce-scatter.7.cloned.1.call-update) | async-done | bytes 1048592 | tf_op jit(solution)/shard_map/reduce_scatter | solution.py:31
  385.4 2.2 reshape.95
  387.6 1.0 copy-done.3
  388.7 7.7 %all-to-all-start.3 = ((bf16[32,4,4096]{2,1,0:T(4,128)(2,1)}), bf16[32,4,4096]{2,1,0:T(4,128)(2,1)S(1)}, u32[]{:S(2)}, u32[]{:S(2)}) async-start(bf16[32,4,4096]{2,1,0:T(4,128)(2,1)} %reshape.95), calls=%async_computation.5 | async-start | bytes 2097152 | tf_op jit(solution)/shard_map/all_to_all | solution.py:35
  396.3 38.2 %reduce-scatter.5.cloned.1.call-done = bf16[128,4096]{1,0:T(8,128)(2,1)} async-done(((bf16[512,4096]{1,0:T(8,128)(2,1)}), bf16[128,4096]{1,0:T(8,128)(2,1)}) %reduce-scatter.5.cloned.1.call-update) | async-done | bytes 1048592 | tf_op jit(solution)/shard_map/reduce_scatter | solution.py:31
  434.5 2.2 reshape.91
  436.8 7.7 %all-to-all-start.1 = ((bf16[32,4,4096]{2,1,0:T(4,128)(2,1)}), bf16[32,4,4096]{2,1,0:T(4,128)(2,1)}, u32[]{:S(2)}, u32[]{:S(2)}) async-start(bf16[32,4,4096]{2,1,0:T(4,128)(2,1)} %reshape.91), calls=%async_computation.2 | async-start | bytes 2097152 | tf_op jit(solution)/shard_map/all_to_all | solution.py:35
  444.5 0.9 convolution_bitcast_fusion
  445.4 2.2 convolution_bitcast_fusion.2
  447.6 1.9 fusion.8
  449.5 11.9 %all-to-all-done.1 = bf16[32,4,4096]{2,1,0:T(4,128)(2,1)} async-done(((bf16[32,4,4096]{2,1,0:T(4,128)(2,1)}), bf16[32,4,4096]{2,1,0:T(4,128)(2,1)}, u32[]{:S(2)}, u32[]{:S(2)}) %all-to-all-start.1) | async-done | bytes 1048608 | tf_op jit(solution)/shard_map/all_to_all | solution.py:35
  461.4 4.6 fusion.22
  (38 shorter events, 0.8 us)
Async XLA Ops:
  7.2 2.1 copy-start
  7.2 103.0 %all-gather.7.cloned.1.call-start = ((), (), s32[]{:S(2)}) async-start(), calls=%async_computation.14 | async-start | bytes 5242880 | tf_op jit(solution)/shard_map/all_gather | solution.py:27
  10.7 30.2 %copy-start.2 = (bf16[128,4096]{1,0:T(8,128)(2,1)S(1)}, bf16[128,4096]{1,0:T(8,128)(2,1)}, u32[]{:S(2)}) copy-start(bf16[128,4096]{1,0:T(8,128)(2,1)} %param.6) | copy-start | bytes 3145732
  10.7 30.2 %copy-start.5 = (f32[128]{0:T(128)S(1)}, f32[128]{0:T(128)}, u32[]{:S(2)}) copy-start(f32[128]{0:T(128)} %param.8) | copy-start | bytes 1540
  40.8 96.2 %all-gather.11.cloned.1.call-start = ((), (), s32[]{:S(2)}) async-start(), calls=%async_computation.18 | async-start | bytes 5242880 | tf_op jit(solution)/shard_map/all_gather | solution.py:27
  64.6 123.3 %all-gather.5.cloned.1.call-start = ((), (), s32[]{:S(2)}) async-start(), calls=%async_computation.12 | async-start | bytes 5242880 | tf_op jit(solution)/shard_map/all_gather | solution.py:27
  87.3 150.7 %all-gather.9.cloned.1.call-start = ((), (), s32[]{:S(2)}) async-start(), calls=%async_computation.16 | async-start | bytes 5242880 | tf_op jit(solution)/shard_map/all_gather | solution.py:27
  110.1 177.4 %reduce-scatter.11.cloned.1.call-start = ((), (), s32[]{:S(2)}) async-start(), calls=%async_computation.19 | async-start | bytes 5242880 | tf_op jit(solution)/shard_map/reduce_scatter | solution.py:31
  150.8 185.7 %reduce-scatter.9.cloned.1.call-start = ((), (), s32[]{:S(2)}) async-start(), calls=%async_computation.17 | async-start | bytes 5242880 | tf_op jit(solution)/shard_map/reduce_scatter | solution.py:31
  251.8 133.6 %reduce-scatter.7.cloned.1.call-start = ((), (), s32[]{:S(2)}) async-start(), calls=%async_computation.15 | async-start | bytes 5242880 | tf_op jit(solution)/shard_map/reduce_scatter | solution.py:31
  258.6 175.9 %reduce-scatter.5.cloned.1.call-start = ((), (), s32[]{:S(2)}) async-start(), calls=%async_computation.13 | async-start | bytes 5242880 | tf_op jit(solution)/shard_map/reduce_scatter | solution.py:31
  289.7 49.0 %all-to-all-start.7 = ((bf16[32,4,4096]{2,1,0:T(4,128)(2,1)}), bf16[32,4,4096]{2,1,0:T(4,128)(2,1)S(1)}, u32[]{:S(2)}, u32[]{:S(2)}) async-start(bf16[32,4,4096]{2,1,0:T(4,128)(2,1)} %reshape.101), calls=%async_computation.11 | async-start | bytes 2097152 | tf_op jit(solution)/shard_map/all_to_all | solution.py:35
  338.7 48.9 %all-to-all-start.5 = ((bf16[32,4,4096]{2,1,0:T(4,128)(2,1)}), bf16[32,4,4096]{2,1,0:T(4,128)(2,1)S(1)}, u32[]{:S(2)}, u32[]{:S(2)}) async-start(bf16[32,4,4096]{2,1,0:T(4,128)(2,1)} %reshape.98), calls=%async_computation.8 | async-start | bytes 2097152 | tf_op jit(solution)/shard_map/all_to_all | solution.py:35
  387.6 1.0 copy-start.3
  388.7 48.1 %all-to-all-start.3 = ((bf16[32,4,4096]{2,1,0:T(4,128)(2,1)}), bf16[32,4,4096]{2,1,0:T(4,128)(2,1)S(1)}, u32[]{:S(2)}, u32[]{:S(2)}) async-start(bf16[32,4,4096]{2,1,0:T(4,128)(2,1)} %reshape.95), calls=%async_computation.5 | async-start | bytes 2097152 | tf_op jit(solution)/shard_map/all_to_all | solution.py:35
  436.8 24.7 %all-to-all-start.1 = ((bf16[32,4,4096]{2,1,0:T(4,128)(2,1)}), bf16[32,4,4096]{2,1,0:T(4,128)(2,1)}, u32[]{:S(2)}, u32[]{:S(2)}) async-start(bf16[32,4,4096]{2,1,0:T(4,128)(2,1)} %reshape.91), calls=%async_computation.2 | async-start | bytes 2097152 | tf_op jit(solution)/shard_map/all_to_all | solution.py:35
  444.5 3.2 copy-start.4
  445.4 20.6 %copy-start.1 = (bf16[128,4096]{1,0:T(8,128)(2,1)S(1)}, bf16[128,4096]{1,0:T(8,128)(2,1)}, u32[]{:S(2)}) copy-start(bf16[128,4096]{1,0:T(8,128)(2,1)} %param.5) | copy-start | bytes 3145732
Sparse Core Ops, SparseCore 0:
  40.9 45.7 all-gather.6
  88.4 48.5 all-gather.10
  139.3 48.5 all-gather.4
  189.4 48.5 all-gather.8
  240.3 47.1 reduce-scatter.10
  289.9 46.5 reduce-scatter.8
  338.9 46.4 reduce-scatter.6
  387.9 46.5 reduce-scatter.4
where the time goes:
time: 474 us; the launch traced here: 473 us
  waiting for transfers between devices  247 us (52%)
  blocking collectives  88.6 us (19%)
  matrix products  70.8 us (15%)
  starting transfers between devices  31.2 us (7%)
  local copies, waits for them, and re-layouts  19.1 us (4%)
  between operations  14.4 us (3%)
    reduce_scatter x4, waiting for transfers between devices, group_sum(): lax.psum_scatter(values.astype(jnp.bfloat16), 'dp', scatter_dimension=0,...  138 us
    all_gather x4, waiting for transfers between devices, group_rows(): return lax.all_gather(values, 'dp', axis=0, tiled=True)  96.4 us
    all_to_all x4, blocking collectives, exchange(): lax.all_to_all(rows.reshape(experts, -1, model_width), 'expert', split_ax...  88.6 us
    all_to_all x4, starting transfers between devices, exchange(): lax.all_to_all(rows.reshape(experts, -1, model_width), 'expert', split_ax...  30.7 us
    dot_general x2, matrix products, forward_rows(): jnp.einsum('rd,kfd->krf', row_block, matrices[:2], preferred_element_type...  17.4 us
    dot_general x2, matrix products, backward_rows(): jnp.einsum('krf,kfd->rd', both_grads, matrices[:2], preferred_element_typ...  15.5 us
    dot_general x2, matrix products, forward_rows(): jnp.dot(hidden, matrices[2], preferred_element_type=jnp.float32)  13.5 us
    reshape x8, local copies, waits for them, and re-layouts, exchange(): rows.reshape(experts, -1, model_width)  12.6 us
  transfers between devices with their start and end apart: 12, of which 8 were waited for; matrix products, arithmetic and copies ran while one was open for 17% of the time, Pallas kernels for 0%

commit v1 on v0

--- a/solution.py
+++ b/solution.py
@@ -2,6 +2,27 @@
 import jax.numpy as jnp
 from jax import lax
 from jax.sharding import PartitionSpec as P
+
+
+def gather_around(x, axis, dim):
+    size, index, rows = (lax.axis_size(axis), lax.axis_index(axis), x.shape[dim])
+    upward = [(i, (i + 1) % size) for i in range(size)]
+    downward = [(i, (i - 1) % size) for i in range(size)]
+    out = jnp.zeros((*x.shape[:dim], size * rows, *x.shape[dim + 1 :]), x.dtype)
+    out = lax.dynamic_update_slice_in_dim(out, x, index * rows, axis=dim)
+    from_left = from_right = x
+    halfway = size // 2
+    for turn in range(1, halfway + 1):
+        from_left = lax.ppermute(from_left, axis, upward)
+        out = lax.dynamic_update_slice_in_dim(
+            out, from_left, (index - turn) % size * rows, axis=dim
+        )
+        if turn < size - halfway:
+            from_right = lax.ppermute(from_right, axis, downward)
+            out = lax.dynamic_update_slice_in_dim(
+                out, from_right, (index + turn) % size * rows, axis=dim
+            )
+    return out
 
 
 def placement(member, slot_count):
@@ -24,7 +45,7 @@
 
 
 def group_rows(values):
-    return lax.all_gather(values, "dp", axis=0, tiled=True)
+    return gather_around(values, "dp", 0)
 
 
 def group_sum(values):

time: 474 us -> 510 us (1.076)
  waiting for transfers between devices: 247 us -> 287 us
  matrix products: 70.8 us -> 51.4 us
  blocking collectives: 88.6 us -> 98.9 us
    ppermute x0 -> x12, waiting for transfers between devices: none -> 231 us  [the longest x8 231 us: gather_around(): from_left = lax.ppermute(from_left, axis, upward)]
    reduce_scatter x4, waiting for transfers between devices: 138 us -> 0.08 us  [group_sum(): lax.psum_scatter(values.astype(jnp.bfloat16), 'dp', scatter_dimension=0,...]
    all_gather x4 -> x0, waiting for transfers between devices: 96.4 us -> none  [group_rows(): return lax.all_gather(values, 'dp', axis=0, tiled=True)]
    all_to_all x4, waiting for transfers between devices: 11.9 us -> 55 us  [exchange(): lax.all_to_all(rows.reshape(experts, -1, model_width), 'expert', split_ax...]
    ppermute x0 -> x12, starting transfers between devices: none -> 11.1 us  [the longest x4 9.47 us: gather_around(): from_right = lax.ppermute(from_right, axis, downward)]
    all_to_all x4, blocking collectives: 88.6 us -> 98.9 us  [exchange(): lax.all_to_all(rows.reshape(experts, -1, model_width), 'expert', split_ax...]
    all_to_all x4, starting transfers between devices: 30.7 us -> 20.7 us  [exchange(): lax.all_to_all(rows.reshape(experts, -1, model_width), 'expert', split_ax...]
    dot_general x2, matrix products: 17.4 us -> 10.2 us  [forward_rows(): jnp.einsum('rd,kfd->krf', row_block, matrices[:2], preferred_element_type...]
  transfers between devices with their start and end apart: 12 -> 20, of which waited for: 8 -> 12; matrix products, arithmetic and copies ran while one was open for 17% -> 11% of each run, Pallas kernels for 0% -> 0%
where the time goes in v1:
time: 510 us; the launch traced here: 509 us
  waiting for transfers between devices  287 us (56%)
  blocking collectives  98.9 us (19%)
  matrix products  51.4 us (10%)
  starting transfers between devices  32 us (6%)
  local copies, waits for them, and re-layouts  23.8 us (5%)
  between operations  14.4 us (3%)
    ppermute x8, waiting for transfers between devices, gather_around(): from_left = lax.ppermute(from_left, axis, upward)  231 us
    all_to_all x4, blocking collectives, exchange(): lax.all_to_all(rows.reshape(experts, -1, model_width), 'expert', split_ax...  98.9 us
    all_to_all x4, waiting for transfers between devices, exchange(): lax.all_to_all(rows.reshape(experts, -1, model_width), 'expert', split_ax...  55 us
    all_to_all x4, starting transfers between devices, exchange(): lax.all_to_all(rows.reshape(experts, -1, model_width), 'expert', split_ax...  20.7 us
    reshape x8, local copies, waits for them, and re-layouts, exchange(): rows.reshape(experts, -1, model_width)  10.7 us
    dot_general x2, matrix products, forward_rows(): jnp.dot(hidden, matrices[2], preferred_element_type=jnp.float32)  10.6 us
    dot_general x2, matrix products, forward_rows(): jnp.einsum('rd,kfd->krf', row_block, matrices[:2], preferred_element_type...  10.2 us
  transfers between devices with their start and end apart: 20, of which 12 were waited for; matrix products, arithmetic and copies ran while one was open for 11% of the time, Pallas kernels for 0%

profile of v1, /device:TPU:1, one launch (start us, length us, event | category | flops | bytes accessed | tf_op | source)
XLA Modules:
  0.0 509.0 jit_solution(14484432593515155934)
XLA Ops:
  10.2 26.3 %all_to_all.40 = bf16[32,4,4096]{2,1,0:T(4,128)(2,1)S(1)} all-to-all(bf16[32,4,4096]{2,1,0:T(4,128)(2,1)S(1)} %reshape.93), channel_id=1, replica_groups=mesh['dp'=4,'expert'=32] {'expert'}, dimensions={0} | all-to-all | bytes 2097152 | tf_op jit(solution)/shard_map/all_to_all | solution.py:56
  36.7 1.3 collective-permute-start.3
  38.0 1.5 collective-permute-start.4
  39.5 23.2 %collective-permute-done.3 = bf16[128,4096]{1,0:T(8,128)(2,1)S(1)} collective-permute-done((bf16[128,4096]{1,0:T(8,128)(2,1)S(1)}, bf16[128,4096]{1,0:T(8,128)(2,1)S(1)}, u32[]{:S(2)}, u32[]{:S(2)}) %collective-permute-start.3) | collective-permute-done | bytes 1048608 | tf_op jit(solution)/shard_map/ppermute | solution.py:16
  63.5 1.7 constant_dynamic-update-slice_fusion.8
  65.2 22.4 %collective-permute-done.5 = bf16[128,4096]{1,0:T(8,128)(2,1)S(1)} collective-permute-done((bf16[128,4096]{1,0:T(8,128)(2,1)S(1)}, bf16[128,4096]{1,0:T(8,128)(2,1)S(1)}, u32[]{:S(2)}, u32[]{:S(2)}) %collective-permute-start.5) | collective-permute-done | bytes 1048608 | tf_op jit(solution)/shard_map/ppermute | solution.py:16
  87.7 3.5 fusion.32
  91.2 1.2 copy-done.9
  92.3 4.3 convolution_convert_fusion
  97.6 22.1 %all_to_all.41 = bf16[32,4,4096]{2,1,0:T(4,128)(2,1)S(1)} all-to-all(bf16[32,4,4096]{2,1,0:T(4,128)(2,1)S(1)} %reshape.89), channel_id=1, replica_groups=mesh['dp'=4,'expert'=32] {'expert'}, dimensions={0} | all-to-all | bytes 2097152 | tf_op jit(solution)/shard_map/all_to_all | solution.py:56
  120.1 2.7 collective-permute-start.1
  122.8 38.8 %collective-permute-done = bf16[128,4096]{1,0:T(8,128)(2,1)S(1)} collective-permute-done((bf16[128,4096]{1,0:T(8,128)(2,1)S(1)}, bf16[128,4096]{1,0:T(8,128)(2,1)S(1)}, u32[]{:S(2)}, u32[]{:S(2)}) %collective-permute-start) | collective-permute-done | bytes 1048608 | tf_op jit(solution)/shard_map/ppermute | solution.py:16
  162.4 24.5 %collective-permute-done.2 = bf16[128,4096]{1,0:T(8,128)(2,1)S(1)} collective-permute-done((bf16[128,4096]{1,0:T(8,128)(2,1)S(1)}, bf16[128,4096]{1,0:T(8,128)(2,1)S(1)}, u32[]{:S(2)}, u32[]{:S(2)}) %collective-permute-start.2) | collective-permute-done | bytes 1048608 | tf_op jit(solution)/shard_map/ppermute | solution.py:16
  187.0 6.7 %fusion.27 = f32[2,512,384]{2,1,0:T(8,128)S(1)} fusion(bf16[1,3,384,4096]{3,2,1,0:T(8,128)(2,1)} %param.9, bf16[512,4096]{1,0:T(8,128)(2,1)S(1)} %constant_dynamic-update-slice_fusion.11), kind=kOutput, calls=%fused_computation.42 | convolution fusion | flops 3221225472 | bytes 12058624 | tf_op jit(solution)/shard_map/rd,kfd->krf/dot_general | solution.py:62
  193.8 1.1 copy-done.7
  194.9 6.3 %convolution_convert_fusion.1 = bf16[512,4096]{1,0:T(8,128)(2,1)} fusion(bf16[1,3,384,4096]{3,2,1,0:T(8,128)(2,1)} %param.9, f32[2,512,384]{2,1,0:T(8,128)S(1)} %fusion.27), kind=kOutput, calls=%fused_computation.9 | convolution fusion | flops 1613889536 | bytes 8912896 | tf_op jit(solution)/shard_map/dot_general | solution.py:66
  201.3 1.1 copy-done.2
  203.4 25.2 %all_to_all.42 = bf16[32,4,4096]{2,1,0:T(4,128)(2,1)} all-to-all(bf16[32,4,4096]{2,1,0:T(4,128)(2,1)S(1)} %reshape.99), channel_id=1, replica_groups=mesh['dp'=4,'expert'=32] {'expert'}, dimensions={0} | all-to-all | bytes 2097152 | tf_op jit(solution)/shard_map/all_to_all | solution.py:56
  228.6 1.3 reshape.100
  230.1 2.7 collective-permute-start.10
  232.7 36.2 %collective-permute-done.9 = bf16[128,4096]{1,0:T(8,128)(2,1)S(1)} collective-permute-done((bf16[128,4096]{1,0:T(8,128)(2,1)S(1)}, bf16[128,4096]{1,0:T(8,128)(2,1)S(1)}, u32[]{:S(2)}, u32[]{:S(2)}) %collective-permute-start.9) | collective-permute-done | bytes 1048608 | tf_op jit(solution)/shard_map/ppermute | solution.py:16
  269.9 24.5 %collective-permute-done.11 = bf16[128,4096]{1,0:T(8,128)(2,1)S(1)} collective-permute-done((bf16[128,4096]{1,0:T(8,128)(2,1)S(1)}, bf16[128,4096]{1,0:T(8,128)(2,1)S(1)}, u32[]{:S(2)}, u32[]{:S(2)}) %collective-permute-start.11) | collective-permute-done | bytes 1048608 | tf_op jit(solution)/shard_map/ppermute | solution.py:16
  294.5 4.5 fusion.72
  299.1 5.0 bitcast_convert_fusion
  305.1 25.2 %all_to_all.43 = bf16[32,4,4096]{2,1,0:T(4,128)(2,1)} all-to-all(bf16[32,4,4096]{2,1,0:T(4,128)(2,1)S(1)} %reshape.96), channel_id=1, replica_groups=mesh['dp'=4,'expert'=32] {'expert'}, dimensions={0} | all-to-all | bytes 2097152 | tf_op jit(solution)/shard_map/all_to_all | solution.py:56
  330.3 1.4 reshape.97
  331.8 2.7 collective-permute-start.7
  334.5 37.4 %collective-permute-done.6 = bf16[128,4096]{1,0:T(8,128)(2,1)S(1)} collective-permute-done((bf16[128,4096]{1,0:T(8,128)(2,1)S(1)}, bf16[128,4096]{1,0:T(8,128)(2,1)S(1)}, u32[]{:S(2)}, u32[]{:S(2)}) %collective-permute-start.6) | collective-permute-done | bytes 1048608 | tf_op jit(solution)/shard_map/ppermute | solution.py:16
  372.7 24.5 %collective-permute-done.8 = bf16[128,4096]{1,0:T(8,128)(2,1)S(1)} collective-permute-done((bf16[128,4096]{1,0:T(8,128)(2,1)S(1)}, bf16[128,4096]{1,0:T(8,128)(2,1)S(1)}, u32[]{:S(2)}, u32[]{:S(2)}) %collective-permute-start.8) | collective-permute-done | bytes 1048608 | tf_op jit(solution)/shard_map/ppermute | solution.py:16
  397.4 4.5 fusion.71
  402.0 5.0 bitcast_convert_fusion.1
  407.0 2.2 reshape.95
  409.2 8.3 %all-to-all-start.3 = ((bf16[32,4,4096]{2,1,0:T(4,128)(2,1)}), bf16[32,4,4096]{2,1,0:T(4,128)(2,1)S(1)}, u32[]{:S(2)}, u32[]{:S(2)}) async-start(bf16[32,4,4096]{2,1,0:T(4,128)(2,1)} %reshape.95), calls=%async_computation.5 | async-start | bytes 2097152 | tf_op jit(solution)/shard_map/all_to_all | solution.py:56
  417.6 2.2 reshape.91
  419.9 14.6 %all-to-all-done.3 = bf16[32,4,4096]{2,1,0:T(4,128)(2,1)S(1)} async-done(((bf16[32,4,4096]{2,1,0:T(4,128)(2,1)}), bf16[32,4,4096]{2,1,0:T(4,128)(2,1)S(1)}, u32[]{:S(2)}, u32[]{:S(2)}) %all-to-all-start.3) | async-done | bytes 1048608 | tf_op jit(solution)/shard_map/all_to_all | solution.py:56
  434.5 4.0 all-to-all-start.1
  438.5 2.3 reshape.101
  440.8 14.6 %all-to-all-done.1 = bf16[32,4,4096]{2,1,0:T(4,128)(2,1)S(1)} async-done(((bf16[32,4,4096]{2,1,0:T(4,128)(2,1)}), bf16[32,4,4096]{2,1,0:T(4,128)(2,1)S(1)}, u32[]{:S(2)}, u32[]{:S(2)}) %all-to-all-start.1) | async-done | bytes 1048608 | tf_op jit(solution)/shard_map/all_to_all | solution.py:56
  455.4 1.0 copy-done.3
  456.4 4.0 all-to-all-start.7
  460.3 2.2 reshape.98
  462.6 14.6 %all-to-all-done.7 = bf16[32,4,4096]{2,1,0:T(4,128)(2,1)S(1)} async-done(((bf16[32,4,4096]{2,1,0:T(4,128)(2,1)}), bf16[32,4,4096]{2,1,0:T(4,128)(2,1)S(1)}, u32[]{:S(2)}, u32[]{:S(2)}) %all-to-all-start.7) | async-done | bytes 1048608 | tf_op jit(solution)/shard_map/all_to_all | solution.py:56
  477.2 4.4 all-to-all-start.5
  481.7 0.9 convolution_bitcast_fusion.2
  482.6 2.3 convolution_bitcast_fusion
  484.9 2.7 fusion.22
  487.6 11.1 %all-to-all-done.5 = bf16[32,4,4096]{2,1,0:T(4,128)(2,1)} async-done(((bf16[32,4,4096]{2,1,0:T(4,128)(2,1)}), bf16[32,4,4096]{2,1,0:T(4,128)(2,1)}, u32[]{:S(2)}, u32[]{:S(2)}) %all-to-all-start.5) | async-done | bytes 1048608 | tf_op jit(solution)/shard_map/all_to_all | solution.py:56
  498.7 3.8 fusion.8
  (94 shorter events, 10.5 us)
Async XLA Ops:
  7.2 2.1 copy-start
  7.2 399.8 %reduce-scatter.7.cloned.1.call-start = ((), (), s32[]{:S(2)}) async-start(), calls=%async_computation.13 | async-start | bytes 5242880 | tf_op jit(solution)/shard_map/reduce_scatter | solution.py:52
  36.7 25.9 %collective-permute-start.3 = (bf16[128,4096]{1,0:T(8,128)(2,1)S(1)}, bf16[128,4096]{1,0:T(8,128)(2,1)S(1)}, u32[]{:S(2)}, u32[]{:S(2)}) collective-permute-start(bf16[128,4096]{1,0:T(8,128)(2,1)S(1)} %reshape.94), channel_id=1, source_target_pairs={{0,32},{32,64},{64,96},{96,0},{1,33},{33,65},{65,97},{97,1},{2,34}... | collective-permute-start | bytes 3145736 | tf_op jit(solution)/shard_map/ppermute | solution.py:16
  38.0 25.5 %collective-permute-start.4 = (bf16[128,4096]{1,0:T(8,128)(2,1)S(1)}, bf16[128,4096]{1,0:T(8,128)(2,1)}, u32[]{:S(2)}, u32[]{:S(2)}) collective-permute-start(bf16[128,4096]{1,0:T(8,128)(2,1)S(1)} %reshape.94), channel_id=1, source_target_pairs={{0,96},{32,0},{64,32},{96,64},{1,97},{33,1},{65,33},{97,65},{2,98}... | collective-permute-start | bytes 3145736 | tf_op jit(solution)/shard_map/ppermute | solution.py:21
  62.6 24.9 %collective-permute-start.5 = (bf16[128,4096]{1,0:T(8,128)(2,1)S(1)}, bf16[128,4096]{1,0:T(8,128)(2,1)S(1)}, u32[]{:S(2)}, u32[]{:S(2)}) collective-permute-start(bf16[128,4096]{1,0:T(8,128)(2,1)S(1)} %collective-permute-done.3), channel_id=1, source_target_pairs={{0,32},{32,64},{64,96},{96,0},{1,33},{33,65},{65,97},{97,1},{2,34}... | collective-permute-start | bytes 3145736 | tf_op jit(solution)/shard_map/ppermute | solution.py:16
  62.7 24.9 %copy-start.6 = (bf16[1,3,384,4096]{3,2,1,0:T(8,128)(2,1)S(1)}, bf16[1,3,384,4096]{3,2,1,0:T(8,128)(2,1)}, u32[]{:S(2)}) copy-start(bf16[1,3,384,4096]{3,2,1,0:T(8,128)(2,1)} %param.9) | copy-start | bytes 28311556
  91.2 1.2 copy-start.9
  96.7 320.9 %reduce-scatter.5.cloned.1.call-start = ((), (), s32[]{:S(2)}) async-start(), calls=%async_computation.12 | async-start | bytes 5242880 | tf_op jit(solution)/shard_map/reduce_scatter | solution.py:52
  120.0 41.5 %collective-permute-start = (bf16[128,4096]{1,0:T(8,128)(2,1)S(1)}, bf16[128,4096]{1,0:T(8,128)(2,1)S(1)}, u32[]{:S(2)}, u32[]{:S(2)}) collective-permute-start(bf16[128,4096]{1,0:T(8,128)(2,1)S(1)} %reshape.90), channel_id=1, source_target_pairs={{0,32},{32,64},{64,96},{96,0},{1,33},{33,65},{65,97},{97,1},{2,34}... | collective-permute-start | bytes 3145736 | tf_op jit(solution)/shard_map/ppermute | solution.py:16
  120.1 42.2 %collective-permute-start.1 = (bf16[128,4096]{1,0:T(8,128)(2,1)S(1)}, bf16[128,4096]{1,0:T(8,128)(2,1)S(1)}, u32[]{:S(2)}, u32[]{:S(2)}) collective-permute-start(bf16[128,4096]{1,0:T(8,128)(2,1)S(1)} %reshape.90), channel_id=1, source_target_pairs={{0,96},{32,0},{64,32},{96,64},{1,97},{33,1},{65,33},{97,65},{2,98}... | collective-permute-start | bytes 3145736 | tf_op jit(solution)/shard_map/ppermute | solution.py:21
  161.5 25.4 %collective-permute-start.2 = (bf16[128,4096]{1,0:T(8,128)(2,1)S(1)}, bf16[128,4096]{1,0:T(8,128)(2,1)S(1)}, u32[]{:S(2)}, u32[]{:S(2)}) collective-permute-start(bf16[128,4096]{1,0:T(8,128)(2,1)S(1)} %collective-permute-done), channel_id=1, source_target_pairs={{0,32},{32,64},{64,96},{96,0},{1,33},{33,65},{65,97},{97,1},{2,34}... | collective-permute-start | bytes 3145736 | tf_op jit(solution)/shard_map/ppermute | solution.py:16
  193.8 1.1 copy-start.7
  201.2 1.2 copy-start.2
  201.2 1.2 copy-start.5
  201.2 237.2 %reduce-scatter.11.cloned.1.call-start = ((), (), s32[]{:S(2)}) async-start(), calls=%async_computation.15 | async-start | bytes 5242880 | tf_op jit(solution)/shard_map/reduce_scatter | solution.py:52
  230.0 39.0 %collective-permute-start.9 = (bf16[128,4096]{1,0:T(8,128)(2,1)S(1)}, bf16[128,4096]{1,0:T(8,128)(2,1)S(1)}, u32[]{:S(2)}, u32[]{:S(2)}) collective-permute-start(bf16[128,4096]{1,0:T(8,128)(2,1)S(1)} %reshape.100), channel_id=1, source_target_pairs={{0,32},{32,64},{64,96},{96,0},{1,33},{33,65},{65,97},{97,1},{2,34}... | collective-permute-start | bytes 3145736 | tf_op jit(solution)/shard_map/ppermute | solution.py:16
  230.1 39.7 %collective-permute-start.10 = (bf16[128,4096]{1,0:T(8,128)(2,1)S(1)}, bf16[128,4096]{1,0:T(8,128)(2,1)S(1)}, u32[]{:S(2)}, u32[]{:S(2)}) collective-permute-start(bf16[128,4096]{1,0:T(8,128)(2,1)S(1)} %reshape.100), channel_id=1, source_target_pairs={{0,96},{32,0},{64,32},{96,64},{1,97},{33,1},{65,33},{97,65},{2,98}... | collective-permute-start | bytes 3145736 | tf_op jit(solution)/shard_map/ppermute | solution.py:21
  269.0 25.4 %collective-permute-start.11 = (bf16[128,4096]{1,0:T(8,128)(2,1)S(1)}, bf16[128,4096]{1,0:T(8,128)(2,1)S(1)}, u32[]{:S(2)}, u32[]{:S(2)}) collective-permute-start(bf16[128,4096]{1,0:T(8,128)(2,1)S(1)} %collective-permute-done.9), channel_id=1, source_target_pairs={{0,32},{32,64},{64,96},{96,0},{1,33},{33,65},{65,97},{97,1},{2,34}... | collective-permute-start | bytes 3145736 | tf_op jit(solution)/shard_map/ppermute | solution.py:16
  269.5 25.0 %copy-start.10 = (f32[2,512,384]{2,1,0:T(8,128)S(1)}, f32[2,512,384]{2,1,0:T(8,128)}, u32[]{:S(2)}) copy-start(f32[2,512,384]{2,1,0:T(8,128)} %copy-done.9) | copy-start | bytes 4718596
  294.4 4.7 slice-start
  294.5 4.6 slice-start.1
  294.5 4.6 slice-start.2
  304.1 156.2 %reduce-scatter.9.cloned.1.call-start = ((), (), s32[]{:S(2)}) async-start(), calls=%async_computation.14 | async-start | bytes 5242880 | tf_op jit(solution)/shard_map/reduce_scatter | solution.py:52
  331.7 40.1 %collective-permute-start.6 = (bf16[128,4096]{1,0:T(8,128)(2,1)S(1)}, bf16[128,4096]{1,0:T(8,128)(2,1)S(1)}, u32[]{:S(2)}, u32[]{:S(2)}) collective-permute-start(bf16[128,4096]{1,0:T(8,128)(2,1)S(1)} %reshape.97), channel_id=1, source_target_pairs={{0,32},{32,64},{64,96},{96,0},{1,33},{33,65},{65,97},{97,1},{2,34}... | collective-permute-start | bytes 3145736 | tf_op jit(solution)/shard_map/ppermute | solution.py:16
  331.8 40.8 %collective-permute-start.7 = (bf16[128,4096]{1,0:T(8,128)(2,1)S(1)}, bf16[128,4096]{1,0:T(8,128)(2,1)S(1)}, u32[]{:S(2)}, u32[]{:S(2)}) collective-permute-start(bf16[128,4096]{1,0:T(8,128)(2,1)S(1)} %reshape.97), channel_id=1, source_target_pairs={{0,96},{32,0},{64,32},{96,64},{1,97},{33,1},{65,33},{97,65},{2,98}... | collective-permute-start | bytes 3145736 | tf_op jit(solution)/shard_map/ppermute | solution.py:21
  371.8 25.4 %collective-permute-start.8 = (bf16[128,4096]{1,0:T(8,128)(2,1)S(1)}, bf16[128,4096]{1,0:T(8,128)(2,1)S(1)}, u32[]{:S(2)}, u32[]{:S(2)}) collective-permute-start(bf16[128,4096]{1,0:T(8,128)(2,1)S(1)} %collective-permute-done.6), channel_id=1, source_target_pairs={{0,32},{32,64},{64,96},{96,0},{1,33},{33,65},{65,97},{97,1},{2,34}... | collective-permute-start | bytes 3145736 | tf_op jit(solution)/shard_map/ppermute | solution.py:16
  372.3 25.0 %copy-start.8 = (f32[2,512,384]{2,1,0:T(8,128)S(1)}, f32[2,512,384]{2,1,0:T(8,128)}, u32[]{:S(2)}) copy-start(f32[2,512,384]{2,1,0:T(8,128)} %copy-done.7) | copy-start | bytes 4718596
  372.6 29.3 %slice-start.3 = ((s8[9437184]{0:T(1024)(128)(4,1)}), s8[4194304]{0:T(1024)(128)(4,1)S(1)}, s32[]{:S(2)}) async-start(s8[9437184]{0:T(1024)(128)(4,1)} %bitcast.160), calls=%async_computation.19 | async-start | bytes 8388608
  397.4 4.6 slice-start.4
  397.4 4.6 slice-start.5
  409.2 25.3 %all-to-all-start.3 = ((bf16[32,4,4096]{2,1,0:T(4,128)(2,1)}), bf16[32,4,4096]{2,1,0:T(4,128)(2,1)S(1)}, u32[]{:S(2)}, u32[]{:S(2)}) async-start(bf16[32,4,4096]{2,1,0:T(4,128)(2,1)} %reshape.95), calls=%async_computation.5 | async-start | bytes 2097152 | tf_op jit(solution)/shard_map/all_to_all | solution.py:56
  434.5 20.9 %all-to-all-start.1 = ((bf16[32,4,4096]{2,1,0:T(4,128)(2,1)}), bf16[32,4,4096]{2,1,0:T(4,128)(2,1)S(1)}, u32[]{:S(2)}, u32[]{:S(2)}) async-start(bf16[32,4,4096]{2,1,0:T(4,128)(2,1)} %reshape.91), calls=%async_computation.2 | async-start | bytes 2097152 | tf_op jit(solution)/shard_map/all_to_all | solution.py:56
  455.4 1.0 copy-start.3
  456.4 20.9 %all-to-all-start.7 = ((bf16[32,4,4096]{2,1,0:T(4,128)(2,1)}), bf16[32,4,4096]{2,1,0:T(4,128)(2,1)S(1)}, u32[]{:S(2)}, u32[]{:S(2)}) async-start(bf16[32,4,4096]{2,1,0:T(4,128)(2,1)} %reshape.101), calls=%async_computation.11 | async-start | bytes 2097152 | tf_op jit(solution)/shard_map/all_to_all | solution.py:56
  477.2 21.4 %all-to-all-start.5 = ((bf16[32,4,4096]{2,1,0:T(4,128)(2,1)}), bf16[32,4,4096]{2,1,0:T(4,128)(2,1)}, u32[]{:S(2)}, u32[]{:S(2)}) async-start(bf16[32,4,4096]{2,1,0:T(4,128)(2,1)} %reshape.98), calls=%async_computation.8 | async-start | bytes 2097152 | tf_op jit(solution)/shard_map/all_to_all | solution.py:56
  481.7 3.2 copy-start.4
  482.6 19.9 %copy-start.1 = (bf16[128,4096]{1,0:T(8,128)(2,1)S(1)}, bf16[128,4096]{1,0:T(8,128)(2,1)}, u32[]{:S(2)}) copy-start(bf16[128,4096]{1,0:T(8,128)(2,1)} %param.5) | copy-start | bytes 3145732
Sparse Core Ops, SparseCore 0:
  96.8 58.1 reduce-scatter.6
  201.4 58.5 reduce-scatter.4
  304.2 59.6 reduce-scatter.10
  407.1 46.3 reduce-scatter.8
